TPU v7x, 512 devices: a whole 4x4x16 slice. The times are simulated.
512 devices in a mesh: ctx: 64 (over z, y_lo, core), head: 8 (over x, y_hi).
Axes of the slice: x: 4, y: 4 (y_hi: 2, y_lo: 2; y = y_hi * 2 + y_lo), z: 16, core: 2. Of those that a mesh axis runs over, the one named last changes fastest.
Arguments:
- queries_nope: bfloat16 [4096, 8192], P('ctx', 'head'), may hold values from -4 to 4
- queries_rope: bfloat16 [4096, 4096], P('ctx', 'head'), may hold values from -128 to 128
- latents: bfloat16 [4096, 512], P('ctx'), may hold values from -8 to 8
- rope_keys: bfloat16 [4096, 64], P('ctx'), may hold values from -4 to 4
- positions: int32 [4096], P('ctx'), may hold values from 0 to 6143
- key_up: bfloat16 [512, 8192], P(None, 'head'), may hold values from -0.5 to 0.5
- value_up: bfloat16 [512, 8192], P(None, 'head'), may hold values from -0.25 to 0.25
- out_proj: bfloat16 [8192, 3584], P('head', 'ctx'), may hold values from -0.0625 to 0.0625
Outputs:
- attended: bfloat16 [4096, 3584], P('ctx', 'head')
All inputs are finite; a program needn't handle non-finite values.
Results may differ from a plain program's by a relative error of at most 0.014.
The roundings to bfloat16 on the way count: a program that leaves them out, or rounds other values in their place, can miss the bound.
Values may be sent and summed in bfloat16 or wider, within the bound.
No kernel may reach another device: no remote copies, remote signals or barrier semaphores. Data moves between devices by JAX's collectives and lax.ppermute only.
A program may use at most 64 MiB of HBM per device.

v0:
```python
import math
import jax
import jax.numpy as jnp
from jax import lax
from jax.sharding import PartitionSpec as P

LATENT = 512
ROPE = 64
NOPE = 128
VDIM = 128
masked_value = -1e30


def rope_tables(token_pos, width):
    half_width = width // 2
    freqs = jnp.exp(jnp.arange(half_width, dtype=jnp.float32) * (-2.0 * math.log(10000.0) / width))
    angle = token_pos.astype(jnp.float32)[:, None] * freqs[None, :]
    return (jnp.cos(angle), jnp.sin(angle))


def rotate(values, cosine, sine):
    half_width = values.shape[-1] // 2
    first_half = values[..., :half_width]
    second_half = values[..., half_width:]
    cos_part = cosine[:, None, :]
    sin_part = sine[:, None, :]
    return jnp.concatenate(
        [
            first_half * cos_part - second_half * sin_part,
            second_half * cos_part + first_half * sin_part,
        ],
        axis=-1,
    )


def make_update(group, keys, rope_part, key_pos):
    lat_query, rope_query, query_pos = group
    scale = 1.0 / math.sqrt(NOPE + ROPE)

    def update(state):
        peak, totals, summed = state
        scores = jnp.einsum("rl,kl->rk", lat_query, keys, preferred_element_type=jnp.float32)
        scores = scores + jnp.einsum(
            "rl,kl->rk", rope_query, rope_part, preferred_element_type=jnp.float32
        )
        visible = key_pos[None, :] <= query_pos[:, None]
        scores = jnp.where(visible, scores * scale, masked_value)
        new_peak = jnp.maximum(peak, jnp.max(scores, axis=1))
        weights = jnp.where(visible, jnp.exp(scores - new_peak[:, None]), 0.0)
        totals = jnp.sum(weights, axis=1)
        summed = jnp.dot(weights.astype(jnp.bfloat16), keys, preferred_element_type=jnp.float32)
        return (new_peak, totals, summed)

    return update


def unchanged(state):
    return state


def attend(groups, latents, rot_keys, positions):
    initial = tuple(
        (
            (
                jnp.full((group[0].shape[0],), masked_value, jnp.float32),
                jnp.zeros((group[0].shape[0],), jnp.float32),
                jnp.zeros((group[0].shape[0], LATENT), jnp.float32),
            )
            for group in groups
        )
    )
    keys = lax.all_gather(latents, "ctx", axis=0, tiled=True)
    rope_part = lax.all_gather(rot_keys, "ctx", axis=0, tiled=True)
    key_pos = lax.all_gather(positions, "ctx", axis=0, tiled=True)
    earliest = jnp.min(key_pos)
    results = []
    for group, fold_state in zip(groups, initial):
        needed = earliest <= jnp.max(group[2])
        results.append(
            lax.cond(needed, make_update(group, keys, rope_part, key_pos), unchanged, fold_state)
        )
    states = tuple(results)
    return [(state[2] / state[1][:, None]).astype(jnp.bfloat16) for state in states]


def upward(latent_out, value_up, token_count, head_count):
    head_out = jnp.einsum(
        "thl,lhd->thd",
        latent_out.reshape(token_count, head_count, LATENT),
        value_up.reshape(LATENT, head_count, VDIM),
        preferred_element_type=jnp.float32,
    )
    return head_out.astype(jnp.bfloat16).reshape(token_count, head_count * VDIM)


def body(queries_nope, queries_rope, latents, rope_keys, positions, key_up, value_up, out_proj):
    token_count = latents.shape[0]
    head_count = key_up.shape[1] // NOPE
    cosine, sine = rope_tables(positions, ROPE)
    rot_queries = rotate(
        queries_rope.astype(jnp.float32).reshape(token_count, head_count, ROPE), cosine, sine
    ).astype(jnp.bfloat16)
    rot_keys = rotate(rope_keys.astype(jnp.float32)[:, None, :], cosine, sine)[:, 0, :].astype(
        jnp.bfloat16
    )
    lat_queries = jnp.einsum(
        "thn,lhn->thl",
        queries_nope.reshape(token_count, head_count, NOPE),
        key_up.reshape(LATENT, head_count, NOPE),
        preferred_element_type=jnp.float32,
    ).astype(jnp.bfloat16)
    lat_rows = lat_queries.reshape(token_count * head_count, LATENT)
    rope_rows = rot_queries.reshape(token_count * head_count, ROPE)
    groups = [(lat_rows, rope_rows, jnp.repeat(positions, head_count))]
    outcome = attend(groups, latents, rot_keys, positions)
    head_out = upward(outcome[0], value_up, token_count, head_count)
    partial_sums = jnp.dot(
        head_out,
        lax.all_gather(out_proj, "ctx", axis=1, tiled=True),
        preferred_element_type=jnp.float32,
    )
    return lax.psum_scatter(
        partial_sums.astype(jnp.bfloat16), "head", scatter_dimension=1, tiled=True
    )


def solution(mesh):
    in_specs = (
        P("ctx", "head"),
        P("ctx", "head"),
        P("ctx", None),
        P("ctx", None),
        P("ctx"),
        P(None, "head"),
        P(None, "head"),
        P("head", "ctx"),
    )
    out_specs = P("ctx", "head")
    return jax.shard_map(body, mesh=mesh, in_specs=in_specs, out_specs=out_specs, check_vma=False)
```

profile of v0, /device:TPU:2, one launch (start us, length us, event | category | flops | bytes accessed | tf_op | source)
XLA Modules:
  0.0 420.3 jit_solution(58696167406577907)
XLA Ops:
  6.5 0.7 all-gather.4.cloned.1.call-update
  7.3 0.7 all-gather.6.cloned.1.call-update
  8.1 0.7 convert_element_type.38
  8.7 1.0 reshape.142
  9.7 0.8 copy.44
  10.8 75.8 %all-gather = bf16[4096,1,64]{2,1,0:T(2,128)(2,1)S(1)} all-gather(bf16[64,1,64]{2,1,0:T(2,128)(2,1)S(1)} %copy.45), channel_id=2, replica_groups=mesh['ctx'=64,'head'=8] {'ctx'}, dimensions={0}, use_global_device_ids=true | all-gather | bytes 532480 | tf_op jit(solution)/shard_map/all_gather | solution.py:73
  86.6 3.6 copy.46
  90.2 1.3 dynamic-slice
  92.1 0.9 dynamic-update-slice
  93.0 208.6 %all-reduce = s32[4096]{0:T(1024)S(1)} all-reduce(s32[4096]{0:T(1024)S(1)} %dynamic-update-slice), channel_id=1, replica_groups=mesh['ctx'=64,'head'=8] {'ctx'}, use_global_device_ids=true, to_apply=%add | all-reduce | flops 4096 | bytes 32768
  301.6 0.6 reduce_min.9
  302.2 1.4 broadcast_reduce_fusion
  305.0 0.2 multiply_cosine_fusion
  305.5 1.4 fusion.12
  307.0 11.8 %conditional.1 = (f32[512]{0:T(512)S(1)}, f32[512,512]{1,0:T(8,128)S(1)}) conditional(s32[]{:T(128)} %convert_element_type.35, () %tuple.13, (s32[4096]{0:T(1024)S(1)}, s32[64,8]{1,0:T(8,128)S(1)}, bf16[64,8,512]{2,0,1:T(8,128)(2,1)S(1)}, bf16[4096,512]{1,0:T(8,128)(2,1)}, bf16[512,64]{1,0:T(8,128)(2,1)S(1)}, ...), branch_computations={%region_2.0_spmd, %region_3.6_spmd} | conditional | flops 4590665216 | bytes 71440456 | solution.py:80
  307.1 4.7 %fusion.8 = f32[512,4096]{1,0:T(8,128)S(1)} fusion(bf16[4096,512]{1,0:T(8,128)(2,1)} %get-tuple-element.21, bf16[64,8,512]{2,0,1:T(8,128)(2,1)S(1)} %get-tuple-element.60), kind=kOutput, calls=%fused_computation.9 | convolution fusion | flops 2147483648 | bytes 13107200 | tf_op jit(solution)/shard_map/cond/branch_1_fun/rl,kl->rk/dot_general | solution.py:42
  311.8 2.2 fusion.34
  314.0 2.4 fusion.2
  316.4 2.2 fusion.1
  318.9 1.7 fusion.13
  320.7 5.4 %convolution_convert_fusion = bf16[64,3584]{1,0:T(8,128)(2,1)S(1)} fusion(bf16[1024,3584]{0,1:T(8,128)(2,1)} %all-gather.6.cloned.1.call-done, bf16[8,8,8,128]{3,2,1,0:T(8,128)(2,1)S(1)} %fusion.13), kind=kOutput, calls=%fused_computation.14 | convolution fusion | flops 469991424 | bytes 7929856 | tf_op jit(solution)/shard_map/dot_general | solution.py:117
  326.1 1.2 copy.53
  327.4 84.8 %reduce-scatter.4.cloned.1.call-done = bf16[448,64]{1,0:T(8,128)(2,1)} async-done(((bf16[3584,64]{1,0:T(8,128)(2,1)}), bf16[448,64]{1,0:T(8,128)(2,1)}) %reduce-scatter.4.cloned.1.call-update) | async-done | bytes 57360
  412.2 1.6 copy.54
  (26 shorter events, 1.0 us)
Async XLA Ops:
  6.5 298.9 %copy-start = (bf16[512,1024]{1,0:T(8,128)(2,1)S(1)}, bf16[512,1024]{1,0:T(8,128)(2,1)}, u32[]{:S(2)}) copy-start(bf16[512,1024]{1,0:T(8,128)(2,1)} %param.15) | copy-start | bytes 3145732
  6.5 300.4 %copy-start.3 = (s32[64]{0:T(128)S(1)}, s32[64]{0:T(128)}, u32[]{:S(2)}) copy-start(s32[64]{0:T(128)} %param.14) | copy-start | bytes 772
  6.5 300.4 %all-gather.4.cloned.1.call-start = ((), (), s32[]{:S(2)}) async-start(), calls=%async_computation.1 | async-start | bytes 4259840 | tf_op jit(solution)/shard_map/all_gather | solution.py:72
  7.3 313.4 %all-gather.6.cloned.1.call-start = ((), (), s32[]{:S(2)}) async-start(), calls=%async_computation.2 | async-start | bytes 7454720 | tf_op jit(solution)/shard_map/all_gather | solution.py:119
  8.0 404.2 %reduce-scatter.4.cloned.1.call-start = ((), (), s32[]{:S(2)}) async-start(), calls=%async_computation.3 | async-start | bytes 1032192
  307.0 4.8 %copy-start.2 = (bf16[4096,64]{0,1:T(8,128)(2,1)S(1)}, bf16[4096,64]{0,1:T(8,128)(2,1)}, u32[]{:S(2)}) copy-start(bf16[4096,64]{0,1:T(8,128)(2,1)} %get-tuple-element.63) | copy-start | bytes 1572868 | tf_op jit(solution)/shard_map/cond
  311.8 2.2 copy-start.1
Sparse Core Ops, SparseCore 0:
  9.5 128.9 all-gather.3
  140.7 124.4 all-gather.5
  327.5 84.6 reduce-scatter.3
where the time goes:
time: 421 us; the launch traced here: 420 us
  blocking collectives  284 us (67%)
  waiting for transfers between devices  86.3 us (20%)
  matrix products  17.8 us (4%)
  between operations  15.2 us (4%)
  local copies, waits for them, and re-layouts  10.6 us (3%)
  other arithmetic  5.75 us (1%)
    unnamed x1, blocking collectives  209 us
    unnamed x4, waiting for transfers between devices  86.2 us
    all_gather x1, blocking collectives, attend(): rope_part = lax.all_gather(rot_keys, 'ctx', axis=0, tiled=True)  75.8 us
  transfers between devices with their start and end apart: 3, of which 1 were waited for; matrix products, arithmetic and copies ran while one was open for 6% of the time, Pallas kernels for 0%

commit v1 on v0

--- a/solution.py
+++ b/solution.py
@@ -70,7 +70,9 @@
         )
     )
     keys = lax.all_gather(latents, "ctx", axis=0, tiled=True)
-    rope_part = lax.all_gather(rot_keys, "ctx", axis=0, tiled=True)
+    rope_part = jnp.concatenate(
+        lax.all_to_all(jnp.stack([rot_keys] * lax.axis_size("ctx")), "ctx", 0, 0), axis=0
+    )
     key_pos = lax.all_gather(positions, "ctx", axis=0, tiled=True)
     earliest = jnp.min(key_pos)
     results = []

time: 421 us -> 384 us (0.912)
  blocking collectives: 284 us -> 223 us
  starting transfers between devices: 0.08 us -> 17.2 us
  waiting for transfers between devices: 86.3 us -> 95.2 us
    all_gather x1 -> x0, blocking collectives: 75.8 us -> none  [attend(): rope_part = lax.all_gather(rot_keys, 'ctx', axis=0, tiled=True)]
    all_to_all x0 -> x1, starting transfers between devices: none -> 17.1 us  [attend(): lax.all_to_all(jnp.stack([rot_keys] * lax.axis_size('ctx')), 'ctx', 0, 0)]
    unnamed x1, blocking collectives: 209 us -> 223 us
    unnamed x4, waiting for transfers between devices: 86.2 us -> 95.2 us
  transfers between devices with their start and end apart: 3 -> 4, of which waited for: 1 -> 1; matrix products, arithmetic and copies ran while one was open for 6% -> 6% of each run, Pallas kernels for 0% -> 0%
where the time goes in v1:
time: 384 us
  blocking collectives  223 us (58%)
  waiting for transfers between devices  95.2 us (25%)
  matrix products  17.7 us (5%)
  starting transfers between devices  17.2 us (4%)
  between operations  15.2 us (4%)
  local copies, waits for them, and re-layouts  9.57 us (2%)
  other arithmetic  5.69 us (1%)
    unnamed x1, blocking collectives  223 us
    unnamed x4, waiting for transfers between devices  95.2 us
    all_to_all x1, starting transfers between devices, attend(): lax.all_to_all(jnp.stack([rot_keys] * lax.axis_size('ctx')), 'ctx', 0, 0)  17.1 us
    unnamed x12, local copies, waits for them, and re-layouts  8.02 us
  transfers between devices with their start and end apart: 4, of which 1 were waited for; matrix products, arithmetic and copies ran while one was open for 6% of the time, Pallas kernels for 0%

profile of v1, /device:TPU:2, one launch (start us, length us, event | category | flops | bytes accessed | tf_op | source)
XLA Modules:
  0.0 383.6 jit_solution(9646696965460987193)
XLA Ops:
  6.5 0.7 all-gather.3.cloned.1.call-update
  7.3 0.7 all-gather.5.cloned.1.call-update
  8.0 0.7 convert_element_type.40
  8.7 0.8 copy.28
  10.0 1.5 reshape.158
  11.6 17.1 %all-to-all-start = ((bf16[64,2,2048]{2,1,0:T(2,128)(2,1)}), bf16[64,2,2048]{2,1,0:T(2,128)(2,1)S(1)}, u32[]{:S(2)}, u32[]{:S(2)}) async-start(bf16[64,2,2048]{2,1,0:T(2,128)(2,1)} %reshape.158), calls=%async_computation | async-start | bytes 1048576 | tf_op jit(solution)/shard_map/all_to_all | solution.py:74
  28.7 1.0 reshape.150
  29.7 1.3 dynamic-slice
  31.7 0.9 dynamic-update-slice
  32.5 222.9 %all-reduce = s32[4096]{0:T(1024)S(1)} all-reduce(s32[4096]{0:T(1024)S(1)} %dynamic-update-slice), channel_id=1, replica_groups=mesh['ctx'=64,'head'=8] {'ctx'}, use_global_device_ids=true, to_apply=%add | all-reduce | flops 4096 | bytes 32768
  255.4 0.6 reduce_min.9
  256.0 1.4 broadcast_reduce_fusion
  259.2 1.4 fusion.12
  260.6 0.7 reshape.159
  261.4 11.7 %conditional.1 = (f32[512]{0:T(512)S(1)}, f32[512,512]{1,0:T(8,128)S(1)}) conditional(s32[]{:T(128)} %convert_element_type.37, () %tuple.13, (s32[4096]{0:T(1024)S(1)}, s32[64,8]{1,0:T(8,128)S(1)}, bf16[64,8,512]{2,0,1:T(8,128)(2,1)S(1)}, bf16[4096,512]{1,0:T(8,128)(2,1)}, bf16[64,64,64]{2,1,0:T(8,128)(2,1)S(1)}, ...), branch_computations={%region_2.0_spmd, %region_3.6_spmd} | conditional | flops 4590665216 | bytes 69343280 | solution.py:82
  261.5 4.6 %fusion.8 = f32[512,4096]{1,0:T(8,128)S(1)} fusion(bf16[4096,512]{1,0:T(8,128)(2,1)} %get-tuple-element.22, bf16[64,8,512]{2,0,1:T(8,128)(2,1)S(1)} %get-tuple-element.49), kind=kOutput, calls=%fused_computation.9 | convolution fusion | flops 2147483648 | bytes 13107200 | tf_op jit(solution)/shard_map/cond/branch_1_fun/rl,kl->rk/dot_general | solution.py:42
  266.1 2.1 fusion.34
  268.3 2.4 fusion.2
  270.7 2.2 fusion.1
  273.3 1.7 fusion.13
  275.0 5.4 %convolution_convert_fusion = bf16[64,3584]{1,0:T(8,128)(2,1)S(1)} fusion(bf16[1024,3584]{0,1:T(8,128)(2,1)} %all-gather.5.cloned.1.call-done, bf16[8,8,8,128]{3,2,1,0:T(8,128)(2,1)S(1)} %fusion.13), kind=kOutput, calls=%fused_computation.14 | convolution fusion | flops 469991424 | bytes 7929856 | tf_op jit(solution)/shard_map/dot_general | solution.py:119
  280.4 1.2 copy.34
  281.7 93.8 %reduce-scatter.4.cloned.1.call-done = bf16[448,64]{1,0:T(8,128)(2,1)} async-done(((bf16[3584,64]{1,0:T(8,128)(2,1)}), bf16[448,64]{1,0:T(8,128)(2,1)}) %reduce-scatter.4.cloned.1.call-update) | async-done | bytes 57360
  375.5 1.6 copy.35
  (27 shorter events, 1.5 us)
Async XLA Ops:
  6.5 252.6 %copy-start = (bf16[512,1024]{1,0:T(8,128)(2,1)S(1)}, bf16[512,1024]{1,0:T(8,128)(2,1)}, u32[]{:S(2)}) copy-start(bf16[512,1024]{1,0:T(8,128)(2,1)} %param.15) | copy-start | bytes 3145732
  6.5 254.8 %copy-start.2 = (s32[64]{0:T(128)S(1)}, s32[64]{0:T(128)}, u32[]{:S(2)}) copy-start(s32[64]{0:T(128)} %param.14) | copy-start | bytes 772
  6.5 254.7 %all-gather.3.cloned.1.call-start = ((), (), s32[]{:S(2)}) async-start(), calls=%async_computation.2 | async-start | bytes 4259840 | tf_op jit(solution)/shard_map/all_gather | solution.py:72
  7.3 267.7 %all-gather.5.cloned.1.call-start = ((), (), s32[]{:S(2)}) async-start(), calls=%async_computation.3 | async-start | bytes 7454720 | tf_op jit(solution)/shard_map/all_gather | solution.py:121
  11.6 249.0 %all-to-all-start = ((bf16[64,2,2048]{2,1,0:T(2,128)(2,1)}), bf16[64,2,2048]{2,1,0:T(2,128)(2,1)S(1)}, u32[]{:S(2)}, u32[]{:S(2)}) async-start(bf16[64,2,2048]{2,1,0:T(2,128)(2,1)} %reshape.158), calls=%async_computation | async-start | bytes 1048576 | tf_op jit(solution)/shard_map/all_to_all | solution.py:74
  28.7 346.8 %reduce-scatter.4.cloned.1.call-start = ((), (), s32[]{:S(2)}) async-start(), calls=%async_computation.4 | async-start | bytes 1032192
  266.1 2.2 copy-start.1
Sparse Core Ops, SparseCore 0:
  9.5 136.9 all-gather.2
  148.6 124.4 all-gather.4
  281.8 93.5 reduce-scatter.3
